TPU v7x, 128 devices: a whole 4x4x4 slice. The times are simulated.
128 devices in a mesh: req: 16 (over z, x), exp: 8 (over y, core).
Axes of the slice: x: 4, y: 4, z: 4, core: 2. Of those that a mesh axis runs over, the one named last changes fastest.
Arguments:
- tokens: bfloat16 [12288, 2880], P(('req', 'exp')), may hold values from -6 to 6
- attn_gain: float32 [2880], replicated, may hold values from 0.5 to 8
- w_query: bfloat16 [2880, 4096], P(None, 'exp'), may hold values from -0.109375 to 0.109375
- key_weight: bfloat16 [2880, 512], P(None, 'exp'), may hold values from -0.109375 to 0.109375
- value_weight: bfloat16 [2880, 512], P(None, 'exp'), may hold values from -0.109375 to 0.109375
- sinks: float32 [64], P('exp'), may hold values from -1 to 3
- w_out: bfloat16 [4096, 2880], P('exp'), may hold values from -0.09375 to 0.09375
- ffn_gain: float32 [2880], replicated, may hold values from 0.25 to 1.75
- router: bfloat16 [2880, 32], replicated, may hold values from -0.109375 to 0.109375
- routes: int32 [12288, 4], P(('req', 'exp')), may hold values from 0 to 31, all different within a row; in each aligned block of 96 rows (0 to 95, 96 to 191, ...) at most 14 rows name the same one
- lengths: int32 [16, 6], P('req'), may hold values from 1 to 384, 768 in all within a row
- expert_gate: bfloat16 [128, 2880, 720], P(('req', 'exp')), may hold values from -0.109375 to 0.109375
- expert_up: bfloat16 [128, 2880, 720], P(('req', 'exp')), may hold values from -0.109375 to 0.109375
- expert_down: bfloat16 [128, 720, 2880], P(('req', 'exp')), may hold values from -0.109375 to 0.109375
Outputs:
- layer_out: bfloat16 [12288, 2880], P(('req', 'exp'))
Inputs may be any that keep to these rules, and one draw needn't show every extreme that they name: `routes`: in the rows of one device no expert is named by more than 14 rows, a bound that some block reaches; a row names 4 different experts.
All inputs are finite; a program needn't handle non-finite values.
Results may differ from a plain program's by a relative error of at most 0.02.
The roundings to bfloat16 on the way count: a program that leaves them out, or rounds other values in their place, can miss the bound.
Values may be sent and summed in bfloat16 or wider, within the bound.
No kernel may reach another device: no remote copies, remote signals or barrier semaphores. Data moves between devices by JAX's collectives and lax.ppermute only.
A program may use at most 192 MiB of HBM per device.

v0:
```python
import jax
import jax.numpy as jnp
from jax import lax
from jax.sharding import PartitionSpec as P

QUERY_HEADS = 64
KEY_VALUE_HEADS = 8
HEAD_DIM = 64
EXPERTS = 32
TOPK = 4
CAP = 14


def rms_norm(value_rows, gain):
    mean_sq = jnp.mean(value_rows * value_rows, axis=-1, keepdims=True)
    return value_rows * lax.rsqrt(mean_sq + 1e-05) * gain


def rotate(value_rows, offset):
    half = value_rows.shape[-1] // 2
    freqs = jnp.exp(
        -(2.0 * jnp.arange(half, dtype=jnp.float32) / value_rows.shape[-1])
        * jnp.log(jnp.float32(150000.0))
    )
    angle = offset.astype(jnp.float32)[:, None] * freqs[None, :]
    cosine = jnp.cos(angle)[:, None, :]
    sine = jnp.sin(angle)[:, None, :]
    first = value_rows[..., :half]
    second = value_rows[..., half:]
    return jnp.concatenate(
        [first * cosine - second * sine, second * cosine + first * sine], axis=-1
    )


def per_device(
    tokens,
    attn_gain,
    w_query,
    key_weight,
    value_weight,
    sinks,
    w_out,
    ffn_gain,
    router,
    routes,
    lengths,
    expert_gate,
    expert_up,
    expert_down,
):
    tok_rows = tokens.shape[0]
    model_width = tokens.shape[1]
    local_heads = w_query.shape[1] // HEAD_DIM
    local_kv = key_weight.shape[1] // HEAD_DIM
    head_group = QUERY_HEADS // KEY_VALUE_HEADS
    normed_input = rms_norm(tokens.astype(jnp.float32), attn_gain).astype(jnp.bfloat16)
    piece = lax.all_gather(normed_input, "exp", axis=0, tiled=True)
    projected = jnp.concatenate(
        [
            jnp.dot(piece, w_query, preferred_element_type=jnp.float32),
            jnp.dot(piece, key_weight, preferred_element_type=jnp.float32),
            jnp.dot(piece, value_weight, preferred_element_type=jnp.float32),
        ],
        axis=1,
    )
    item_count = projected.shape[0]
    lens = lengths[0]
    ends = jnp.cumsum(lens)
    starts = ends - lens
    position = jnp.arange(item_count, dtype=jnp.int32)
    member = ((position[:, None] >= starts[None, :]) & (position[:, None] < ends[None, :])).astype(
        jnp.int32
    )
    segment = jnp.sum(member * jnp.arange(lens.shape[0], dtype=jnp.int32)[None, :], axis=1)
    offset = position - jnp.sum(member * starts[None, :], axis=1)
    q_width = local_heads * HEAD_DIM
    kv_width = local_kv * HEAD_DIM
    query_rows = rotate(
        projected[:, :q_width].reshape(item_count, local_heads, HEAD_DIM), offset
    ).astype(jnp.bfloat16)
    key_rows = rotate(
        projected[:, q_width : q_width + kv_width].reshape(item_count, local_kv, HEAD_DIM), offset
    ).astype(jnp.bfloat16)
    value_rows = (
        projected[:, q_width + kv_width :]
        .reshape(item_count, local_kv, HEAD_DIM)
        .astype(jnp.bfloat16)
    )
    grouped_heads = query_rows.reshape(item_count, local_kv, head_group, HEAD_DIM)
    scores = jnp.einsum(
        "qcgd,kcd->cgqk", grouped_heads, key_rows, preferred_element_type=jnp.float32
    ) * HEAD_DIM ** (-0.5)
    allowed = (segment[:, None] == segment[None, :]) & (position[None, :] <= position[:, None])
    sink_score_logit = sinks.reshape(local_kv, head_group, 1, 1)
    masked = jnp.where(allowed[None, None], scores, -jnp.inf)
    top = jnp.maximum(jnp.max(masked, axis=-1, keepdims=True), sink_score_logit)
    expo = jnp.where(allowed[None, None], jnp.exp(scores - top), 0.0)
    denom = jnp.sum(expo, axis=-1, keepdims=True) + jnp.exp(sink_score_logit - top)
    probs = (expo / denom).astype(jnp.bfloat16)
    attended = jnp.einsum("cgqk,kcd->qcgd", probs, value_rows, preferred_element_type=jnp.float32)
    attended = attended.reshape(item_count, q_width).astype(jnp.bfloat16)
    attn_sum = lax.psum_scatter(
        jnp.dot(attended, w_out, preferred_element_type=jnp.float32).astype(jnp.bfloat16),
        "exp",
        scatter_dimension=0,
        tiled=True,
    ).astype(jnp.float32)
    residual = (tokens.astype(jnp.float32) + attn_sum).astype(jnp.bfloat16)
    normed2 = rms_norm(residual.astype(jnp.float32), ffn_gain).astype(jnp.bfloat16)
    logits = jnp.dot(normed2, router, preferred_element_type=jnp.float32)
    picked = jnp.take_along_axis(logits, routes, axis=1)
    weights = jax.nn.softmax(picked, axis=-1)
    flat_routes = routes.reshape(-1)
    expert_ids = jnp.arange(EXPERTS, dtype=jnp.int32)
    onehot_route = (flat_routes[:, None] == expert_ids[None, :]).astype(jnp.int32)
    rank = jnp.cumsum(onehot_route, axis=0) - 1
    slot_rank = jnp.sum(onehot_route * rank, axis=1)
    flat_slot = flat_routes * CAP + slot_rank
    slot_ids = jnp.arange(EXPERTS * CAP, dtype=jnp.int32)
    dispatch_table = (slot_ids[:, None] == flat_slot[None, :]).astype(jnp.bfloat16)
    repeated = jnp.repeat(normed2, TOPK, axis=0)
    packed = jnp.dot(dispatch_table, repeated, preferred_element_type=jnp.float32).astype(
        jnp.bfloat16
    )
    n_req = lax.axis_size("req")
    n_exp = lax.axis_size("exp")
    devices = n_req * n_exp
    split = devices // EXPERTS
    send_rows = jnp.broadcast_to(
        packed.reshape(EXPERTS, 1, CAP, model_width), (EXPERTS, split, CAP, model_width)
    ).reshape(devices, CAP, model_width)
    received = lax.all_to_all(send_rows, ("req", "exp"), split_axis=0, concat_axis=0, tiled=True)
    flat_rows = received.reshape(-1, model_width)
    gate = jnp.dot(flat_rows, expert_gate[0], preferred_element_type=jnp.float32)
    up_val = jnp.dot(flat_rows, expert_up[0], preferred_element_type=jnp.float32)
    hidden = ((up_val + 1.0) * gate * jax.nn.sigmoid(1.702 * gate)).astype(jnp.bfloat16)
    slice_out = jnp.dot(hidden, expert_down[0], preferred_element_type=jnp.float32).astype(
        jnp.bfloat16
    )
    returned = lax.all_to_all(
        slice_out.reshape(received.shape), ("req", "exp"), split_axis=0, concat_axis=0, tiled=True
    )
    summed = returned.astype(jnp.float32).reshape(EXPERTS, split, CAP, model_width).sum(axis=1)
    summed = summed.reshape(EXPERTS * CAP, model_width)
    picked_rows = jnp.take(summed, flat_slot, axis=0).reshape(tok_rows, TOPK, model_width)
    moe_sum = jnp.sum(weights[:, :, None] * picked_rows, axis=1)
    return (residual.astype(jnp.float32) + moe_sum).astype(jnp.bfloat16)


def solution(mesh):
    return jax.shard_map(
        per_device,
        mesh=mesh,
        in_specs=(
            P(("req", "exp"), None),
            P(),
            P(None, "exp"),
            P(None, "exp"),
            P(None, "exp"),
            P("exp"),
            P("exp", None),
            P(),
            P(),
            P(("req", "exp"), None),
            P("req", None),
            P(("req", "exp"), None, None),
            P(("req", "exp"), None, None),
            P(("req", "exp"), None, None),
        ),
        out_specs=P(("req", "exp"), None),
        check_vma=False,
    )
```

profile of v0, /device:TPU:14, one launch (start us, length us, event | category | flops | bytes accessed | tf_op | source)
XLA Modules:
  0.0 587.9 jit_solution(4064006883043466249)
XLA Ops:
  6.5 1.4 fusion.19
  8.0 2.1 fusion.21
  10.0 0.0 all-gather.2.cloned.1.call-update
  10.1 0.0 reduce-scatter.2.cloned.1.call-start
  10.1 0.8 reduce-window.10
  11.0 0.7 fusion.52
  11.6 0.1 select_reduce_fusion.1
  11.7 1.1 multiply_cosine_fusion
  12.8 0.4 fusion.13
  13.2 31.8 %all-gather.2.cloned.1.call-done = bf16[768,2880]{1,0:T(8,128)(2,1)} async-done(((bf16[96,2880]{1,0:T(8,128)(2,1)}), bf16[768,2880]{1,0:T(8,128)(2,1)}) %all-gather.2.cloned.1.call-update) | async-done | bytes 4423696 | tf_op jit(solution)/shard_map/all_gather | solution.py:57
  45.0 3.9 convolution_bitcast_fusion
  48.9 0.4 fusion.46
  49.4 4.6 fusion.59
  54.0 0.2 subtract_convert_fusion
  54.2 0.0 copy-start.11
  54.2 8.6 %fusion = (f32[8,768]{1,0:T(8,128)S(1)}, f32[768,768,8]{1,0,2:T(8,128)}) fusion(pred[768,768]{0,1:T(8,128)(4,1)S(1)} %fusion.13, bf16[768,8,32]{0,2,1:T(8,128)(2,1)S(1)} %get-tuple-element.10, bf16[768,8,32]{0,2,1:T(8,128)(2,1)S(1)} %get-tuple-element.9, bf16[768,32]{0,1:T(8,128)(2,1)S(1)} %get-tuple-element.12, bf16[768,32]{0,1:T(8,128)(2,1)S(1)} %get-tuple-element.11), kind=kOutput, calls=%fused_computation.5 | convolution fusion | flops 619898880 | bytes 20373504 | tf_op jit(solution)/shard_map/qcgd,kcd->cgqk/dot_general | solution.py:90
  62.9 0.6 copy-done.7
  63.5 0.7 broadcast_maximum_fusion
  64.2 10.8 %fusion.3 = f32[8,768]{1,0:T(8,128)} fusion(f32[768,768,8]{1,0,2:T(8,128)} %get-tuple-element.16, f32[8,768]{1,0:T(8,128)} %broadcast_maximum_fusion, pred[768,768]{0,1:T(8,128)(4,1)S(1)} %fusion.13), kind=kLoop, calls=%fused_computation.9 | loop fusion | flops 18868224 | bytes 19513344 | tf_op jit(solution)/shard_map/reduce_sum | solution.py:98
  75.0 1.4 exponential_add_fusion
  76.4 14.1 %fusion.16 = bf16[64,8,768]{2,0,1:T(8,128)(2,1)} fusion(f32[8,768]{1,0:T(8,128)} %exponential_add_fusion, f32[8,768]{1,0:T(8,128)} %broadcast_maximum_fusion, f32[768,768,8]{1,0,2:T(8,128)} %get-tuple-element.16, pred[768,768]{0,1:T(8,128)(4,1)S(1)} %fusion.13, bf16[768,2880]{1,0:T(8,128)(2,1)} %all-gather.2.cloned.1.call-done, bf16[2880,64]{0,1:T(8,128)(2,1)} %param.18), kind=kOutput, calls=%fused_computation.30 | convolution fusion | flops 911130624 | bytes 25092096 | tf_op jit(solution)/shard_map/cgqk,kcd->qcgd/dot_general | solution.py:100
  90.5 5.8 convolution_convert_fusion.1
  96.3 0.0 reduce-scatter.2.cloned.1.call-update
  96.3 0.7 copy-done.9
  97.0 0.1 copy.44
  97.1 0.1 reshape.415
  97.2 0.1 eq.59
  97.3 1.0 reduce-window.11
  98.4 0.2 slice_reduce_fusion
  98.6 0.1 fusion.44
  98.7 33.6 %reduce-scatter.2.cloned.1.call-done = bf16[96,2880]{1,0:T(8,128)(2,1)} async-done(((bf16[768,2880]{1,0:T(8,128)(2,1)}), bf16[96,2880]{1,0:T(8,128)(2,1)}) %reduce-scatter.2.cloned.1.call-update) | async-done | bytes 552976 | tf_op jit(solution)/shard_map/reduce_scatter | solution.py:102
  132.4 1.3 fusion.23
  133.7 1.3 fusion.25
  135.0 0.6 broadcast_in_dim.40
  135.6 2.4 reshape.417
  138.1 4.7 convolution_convert_fusion.2
  142.8 4.4 broadcast_in_dim.41
  147.2 7.1 %broadcast_in_dim.42 = bf16[32,4,14,2880]{3,2,1,0:T(8,128)(2,1)} broadcast(bf16[32,14,2880]{2,1,0:T(8,128)(2,1)} %broadcast_in_dim.41), dimensions={0,2,3} | broadcast | bytes 12902400 | tf_op jit(solution)/shard_map/broadcast_in_dim | solution.py:129
  154.3 146.0 %all_to_all.10 = bf16[128,14,2880]{2,1,0:T(8,128)(2,1)} all-to-all(bf16[128,14,2880]{2,1,0:T(8,128)(2,1)} %bitcast.104), channel_id=1, replica_groups=mesh['req'=16,'exp'=8] {'req','exp'}, dimensions={0} | all-to-all | bytes 20643840 | tf_op jit(solution)/shard_map/all_to_all | solution.py:132
  300.4 15.4 %reshape.419 = bf16[1792,2880]{1,0:T(8,128)(2,1)} reshape(bf16[128,14,2880]{2,1,0:T(8,128)(2,1)} %all_to_all.10) | data formatting | bytes 20643840 | tf_op jit(solution)/shard_map/reshape | solution.py:133
  315.7 14.6 %fusion.7 = f32[1792,720]{0,1:T(8,128)} fusion(bf16[1792,2880]{1,0:T(8,128)(2,1)} %reshape.419, bf16[1,2880,720]{1,2,0:T(8,128)(2,1)} %param.25), kind=kOutput, calls=%fused_computation.18 | convolution fusion | flops 7431782400 | bytes 19630080 | tf_op jit(solution)/shard_map/dot_general | solution.py:134
  330.3 27.2 %convolution_convert_fusion = bf16[1792,2880]{0,1:T(8,128)(2,1)} fusion(bf16[1,720,2880]{2,1,0:T(8,128)(2,1)} %param.27, f32[1792,720]{0,1:T(8,128)} %fusion.7, bf16[1792,2880]{1,0:T(8,128)(2,1)} %reshape.419, bf16[1,2880,720]{1,2,0:T(8,128)(2,1)} %param.26), kind=kOutput, calls=%fused_computation.10 | convolution fusion | flops 14879047680 | bytes 34099200 | tf_op jit(solution)/shard_map/dot_general | solution.py:137
  357.6 14.3 %copy.49 = bf16[1792,2880]{1,0:T(8,128)(2,1)} copy(bf16[1792,2880]{0,1:T(8,128)(2,1)} %convolution_convert_fusion) | data formatting | bytes 20643840 | tf_op jit(solution)/shard_map/convert_element_type | solution.py:137
  371.9 14.4 %reshape.420 = bf16[128,14,2880]{2,1,0:T(8,128)(2,1)} reshape(bf16[1792,2880]{1,0:T(8,128)(2,1)} %copy.49) | data formatting | bytes 20643840 | tf_op jit(solution)/shard_map/reshape | solution.py:141
  386.3 8.2 %all-to-all-start.1 = ((bf16[128,14,2880]{2,1,0:T(8,128)(2,1)}), bf16[128,14,2880]{2,1,0:T(8,128)(2,1)}, u32[]{:S(2)}, u32[]{:S(2)}) async-start(bf16[128,14,2880]{2,1,0:T(8,128)(2,1)} %reshape.420), calls=%async_computation.2 | async-start | bytes 24117248 | tf_op jit(solution)/shard_map/all_to_all | solution.py:140
  394.5 0.1 reduce_sum.92
  394.7 0.1 copy.50
  394.8 0.1 mul.250
  394.9 0.1 copy.41
  395.0 0.1 reshape.434
  395.1 0.1 copy.47
  395.2 0.1 copy.48
  395.4 0.3 fusion.60
  395.7 2.9 gather_fusion.1
  398.6 0.1 reshape.437
  398.7 0.1 copy.42
  398.8 0.7 copy.43
  399.5 143.8 %all-to-all-done.1 = bf16[128,14,2880]{2,1,0:T(8,128)(2,1)} async-done(((bf16[128,14,2880]{2,1,0:T(8,128)(2,1)}), bf16[128,14,2880]{2,1,0:T(8,128)(2,1)}, u32[]{:S(2)}, u32[]{:S(2)}) %all-to-all-start.1) | async-done | bytes 10321952 | tf_op jit(solution)/shard_map/all_to_all | solution.py:140
  543.3 9.8 %convert_reduce_fusion = f32[32,14,2880]{2,1,0:T(8,128)} fusion(bf16[128,14,2880]{2,1,0:T(8,128)(2,1)} %all-to-all-done.1), kind=kLoop, calls=%fused_computation.2 | loop fusion | flops 9031680 | bytes 15482880 | tf_op jit(solution)/shard_map/reduce_sum | solution.py:143
  553.1 5.6 reshape.423
  558.7 9.1 %gather_fusion = f32[384,2880]{1,0:T(8,128)} fusion(f32[448,2880]{1,0:T(8,128)} %reshape.423, s32[1024]{0:T(1024)S(1)} %pad_clamp_fusion), kind=kCustom, calls=%fused_computation | custom fusion | bytes 8848896 | tf_op jit(solution)/shard_map/jit(_take)/gather | solution.py:145
  567.8 5.5 gather.12
  573.3 6.5 %multiply_reduce_fusion = f32[96,2880]{1,0:T(8,128)S(1)} fusion(f32[96,4,2880]{2,1,0:T(4,128)} %gather.12, f32[96,4]{1,0:T(8,128)} %copy.43, pred[96,4]{1,0:T(8,128)(4,1)S(1)} %copy.48), kind=kLoop, calls=%fused_computation.15 | loop fusion | flops 3041280 | bytes 5531520 | tf_op jit(solution)/shard_map/reduce_sum | solution.py:146
  579.9 1.0 fusion.26
  (37 shorter events, 0.2 us)
Async XLA Ops:
  6.5 83.9 %copy-start = (bf16[512,2880]{0,1:T(8,128)(2,1)S(1)}, bf16[512,2880]{0,1:T(8,128)(2,1)}, u32[]{:S(2)}) copy-start(bf16[512,2880]{0,1:T(8,128)(2,1)} %param.20) | copy-start | bytes 8847364
  6.5 38.4 %all-gather.2.cloned.1.call-start = ((), (), s32[]{:S(2)}) async-start(), calls=%async_computation.3 | async-start | bytes 5087232 | tf_op jit(solution)/shard_map/all_gather | solution.py:57
  10.1 122.3 %reduce-scatter.2.cloned.1.call-start = ((), (), s32[]{:S(2)}) async-start(), calls=%async_computation.4 | async-start | bytes 5087232 | tf_op jit(solution)/shard_map/reduce_scatter | solution.py:102
  45.0 4.4 copy-start.4
  49.3 4.7 copy-start.5
  49.3 4.7 copy-start.6
  54.2 9.3 %copy-start.11 = (f32[8]{0:T(128)S(1)}, f32[8]{0:T(128)}, u32[]{:S(2)}) copy-start(f32[8]{0:T(128)} %param.19) | copy-start | bytes 100
  62.9 0.6 copy-start.7
  96.3 0.7 copy-start.9
  96.3 36.1 %copy-start.2 = (bf16[96,2880]{1,0:T(8,128)(2,1)S(1)}, bf16[96,2880]{1,0:T(8,128)(2,1)}, u32[]{:S(2)}) copy-start(bf16[96,2880]{1,0:T(8,128)(2,1)} %param.14) | copy-start | bytes 1658884
  96.3 37.4 %copy-start.10 = (f32[2880]{0:T(1024)S(1)}, f32[2880]{0:T(1024)}, u32[]{:S(2)}) copy-start(f32[2880]{0:T(1024)} %param.21) | copy-start | bytes 34564
  386.3 9.0 %copy-start.8 = (bf16[2880,32]{0,1:T(8,128)(2,1)S(1)}, bf16[2880,32]{0,1:T(8,128)(2,1)}, u32[]{:S(2)}) copy-start(bf16[2880,32]{0,1:T(8,128)(2,1)} %param.22) | copy-start | bytes 552964
  386.3 157.0 %all-to-all-start.1 = ((bf16[128,14,2880]{2,1,0:T(8,128)(2,1)}), bf16[128,14,2880]{2,1,0:T(8,128)(2,1)}, u32[]{:S(2)}, u32[]{:S(2)}) async-start(bf16[128,14,2880]{2,1,0:T(8,128)(2,1)} %reshape.420), calls=%async_computation.2 | async-start | bytes 24117248 | tf_op jit(solution)/shard_map/all_to_all | solution.py:140
  567.8 13.1 %copy-start.1 = (bf16[512,2880]{0,1:T(8,128)(2,1)S(1)}, bf16[512,2880]{0,1:T(8,128)(2,1)}, u32[]{:S(2)}) copy-start(bf16[512,2880]{0,1:T(8,128)(2,1)} %param.20) | copy-start | bytes 8847364
  573.3 6.5 %copy-start.3 = (bf16[96,2880]{1,0:T(8,128)(2,1)S(1)}, bf16[96,2880]{1,0:T(8,128)(2,1)}, u32[]{:S(2)}) copy-start(bf16[96,2880]{1,0:T(8,128)(2,1)} %reduce-scatter.2.cloned.1.call-done) | copy-start | bytes 1658884
Sparse Core Ops, SparseCore 0:
  10.2 34.7 all-gather.1
  96.5 35.8 reduce-scatter.1
where the time goes:
time: 594 us; the launch traced here: 588 us
  waiting for transfers between devices  209 us (35%)
  blocking collectives  146 us (25%)
  local copies, waits for them, and re-layouts  85.3 us (14%)
  matrix products  83.9 us (14%)
  other arithmetic  41.3 us (7%)
  between operations  13.9 us (2%)
  starting transfers between devices  8.24 us (1%)
    all_to_all x1, blocking collectives, per_device(): lax.all_to_all(send_rows, ('req', 'exp'), split_axis=0, concat_axis=0, ti...  146 us
    all_to_all x1, waiting for transfers between devices, per_device(): lax.all_to_all(slice_out.reshape(received.shape), ('req', 'exp'), split_a...  144 us
    reduce_scatter x1, waiting for transfers between devices, per_device(): lax.psum_scatter(jnp.dot(attended, w_out, preferred_element_type=jnp.floa...  33.6 us
    all_gather x1, waiting for transfers between devices, per_device(): piece = lax.all_gather(normed_input, 'exp', axis=0, tiled=True)  31.8 us
    dot_general x1, matrix products, per_device(): jnp.dot(hidden, expert_down[0], preferred_element_type=jnp.float32)  27.2 us
    reshape x1, local copies, waits for them, and re-layouts, per_device(): flat_rows = received.reshape(-1, model_width)  15.4 us
    gather x2, local copies, waits for them, and re-layouts, per_device(): jnp.take(summed, flat_slot, axis=0).reshape(tok_rows, TOPK, model_width)  14.6 us
    dot_general x1, matrix products, per_device(): jnp.dot(flat_rows, expert_gate[0], preferred_element_type=jnp.float32)  14.6 us
  transfers between devices with their start and end apart: 3, of which 3 were waited for; matrix products, arithmetic and copies ran while one was open for 2% of the time, Pallas kernels for 0%

commit v1 on v0

--- a/solution.py
+++ b/solution.py
@@ -1,3 +1,4 @@
+import functools
 import jax
 import jax.numpy as jnp
 from jax import lax
@@ -9,6 +10,18 @@
 EXPERTS = 32
 TOPK = 4
 CAP = 14
+
+
+def view_windows(incoming_x, comm_axis):
+    n_shards = jax.lax.axis_size(comm_axis)
+    v1 = tuple((n_shards if h == 0 else 1 for h in range(incoming_x.ndim)))
+    work_now = jnp.tile(incoming_x, v1)
+    return jax.lax.all_to_all(
+        work_now, axis_name=comm_axis, split_axis=0, concat_axis=0, tiled=True
+    )
+
+
+define_leaves_now = functools.partial(view_windows, comm_axis="exp")
 
 
 def rms_norm(value_rows, gain):
@@ -54,7 +67,7 @@
     local_kv = key_weight.shape[1] // HEAD_DIM
     head_group = QUERY_HEADS // KEY_VALUE_HEADS
     normed_input = rms_norm(tokens.astype(jnp.float32), attn_gain).astype(jnp.bfloat16)
-    piece = lax.all_gather(normed_input, "exp", axis=0, tiled=True)
+    piece = define_leaves_now(normed_input)
     projected = jnp.concatenate(
         [
             jnp.dot(piece, w_query, preferred_element_type=jnp.float32),

time: 594 us -> 622 us (1.047)
  waiting for transfers between devices: 209 us -> 223 us
  local copies, waits for them, and re-layouts: 85.3 us -> 92.3 us
    all_to_all x0 -> x1, waiting for transfers between devices: none -> 45.5 us  [view_windows(): jax.lax.all_to_all(work_now, axis_name=comm_axis, split_axis=0, concat_ax...]
    all_gather x1 -> x0, waiting for transfers between devices: 31.8 us -> none  [per_device(): piece = lax.all_gather(normed_input, 'exp', axis=0, tiled=True)]
where the time goes in v1:
time: 622 us; the launch traced here: 612 us
  waiting for transfers between devices  223 us (36%)
  blocking collectives  146 us (23%)
  local copies, waits for them, and re-layouts  92.3 us (15%)
  matrix products  84.2 us (14%)
  other arithmetic  39 us (6%)
  between operations  13.9 us (2%)
  starting transfers between devices  13.1 us (2%)
    all_to_all x1, blocking collectives, per_device(): lax.all_to_all(send_rows, ('req', 'exp'), split_axis=0, concat_axis=0, ti...  146 us
    all_to_all x1, waiting for transfers between devices, per_device(): lax.all_to_all(slice_out.reshape(received.shape), ('req', 'exp'), split_a...  144 us
    all_to_all x1, waiting for transfers between devices, view_windows(): jax.lax.all_to_all(work_now, axis_name=comm_axis, split_axis=0, concat_ax...  45.5 us
    reduce_scatter x1, waiting for transfers between devices, per_device(): lax.psum_scatter(jnp.dot(attended, w_out, preferred_element_type=jnp.floa...  34.2 us
    dot_general x1, matrix products, per_device(): jnp.dot(hidden, expert_down[0], preferred_element_type=jnp.float32)  27.2 us
    reshape x1, local copies, waits for them, and re-layouts, per_device(): flat_rows = received.reshape(-1, model_width)  15.4 us
    gather x2, local copies, waits for them, and re-layouts, per_device(): jnp.take(summed, flat_slot, axis=0).reshape(tok_rows, TOPK, model_width)  14.6 us
    dot_general x1, matrix products, per_device(): jnp.dot(flat_rows, expert_gate[0], preferred_element_type=jnp.float32)  14.6 us
  transfers between devices with their start and end apart: 3, of which 3 were waited for; matrix products, arithmetic and copies ran while one was open for 2% of the time, Pallas kernels for 0%

profile of v1, /device:TPU:14, one launch (start us, length us, event | category | flops | bytes accessed | tf_op | source)
XLA Modules:
  0.0 612.2 jit_solution(966165134406298358)
XLA Ops:
  6.5 1.4 fusion.19
  8.0 1.3 fusion.21
  9.2 2.4 tile.2
  11.6 4.9 all-to-all-start
  16.5 4.6 copy.46
  21.1 0.2 reduce-window.10
  21.3 0.1 select_reduce_fusion.1
  21.4 1.1 multiply_cosine_fusion
  22.5 0.4 fusion.13
  22.9 45.5 %all-to-all-done = bf16[8,96,2880]{2,1,0:T(8,128)(2,1)} async-done(((bf16[8,96,2880]{2,1,0:T(8,128)(2,1)}), bf16[8,96,2880]{2,1,0:T(8,128)(2,1)}, u32[]{:S(2)}, u32[]{:S(2)}) %all-to-all-start) | async-done | bytes 4423712 | tf_op jit(solution)/shard_map/all_to_all | solution.py:19
  68.4 3.9 convolution_bitcast_fusion
  72.3 0.4 fusion.46
  72.7 0.0 copy-start.5
  72.8 5.0 fusion.59
  77.7 0.2 subtract_convert_fusion
  78.0 8.2 %fusion = (f32[8,768]{1,0:T(8,128)S(1)}, f32[768,768,8]{1,0,2:T(8,128)}) fusion(pred[768,768]{0,1:T(8,128)(4,1)S(1)} %fusion.13, bf16[768,8,32]{0,2,1:T(8,128)(2,1)S(1)} %get-tuple-element.10, bf16[768,8,32]{0,2,1:T(8,128)(2,1)S(1)} %get-tuple-element.9, bf16[768,32]{0,1:T(8,128)(2,1)S(1)} %get-tuple-element.12, bf16[768,32]{0,1:T(8,128)(2,1)S(1)} %get-tuple-element.11), kind=kOutput, calls=%fused_computation.5 | convolution fusion | flops 619898880 | bytes 20373504 | tf_op jit(solution)/shard_map/qcgd,kcd->cgqk/dot_general | solution.py:103
  86.2 0.6 copy-done.7
  86.8 0.7 broadcast_maximum_fusion
  87.4 10.8 %fusion.3 = f32[8,768]{1,0:T(8,128)} fusion(f32[768,768,8]{1,0,2:T(8,128)} %get-tuple-element.16, f32[8,768]{1,0:T(8,128)} %broadcast_maximum_fusion, pred[768,768]{0,1:T(8,128)(4,1)S(1)} %fusion.13), kind=kLoop, calls=%fused_computation.9 | loop fusion | flops 18868224 | bytes 19513344 | tf_op jit(solution)/shard_map/reduce_sum | solution.py:111
  98.2 1.4 exponential_add_fusion
  99.7 14.5 %fusion.16 = bf16[64,8,768]{2,0,1:T(8,128)(2,1)} fusion(f32[8,768]{1,0:T(8,128)} %exponential_add_fusion, f32[8,768]{1,0:T(8,128)} %broadcast_maximum_fusion, f32[768,768,8]{1,0,2:T(8,128)} %get-tuple-element.16, pred[768,768]{0,1:T(8,128)(4,1)S(1)} %fusion.13, bf16[768,2880]{1,0:T(8,128)(2,1)} %bitcast, bf16[2880,64]{0,1:T(8,128)(2,1)} %param.18), kind=kOutput, calls=%fused_computation.30 | convolution fusion | flops 911130624 | bytes 25092096 | tf_op jit(solution)/shard_map/cgqk,kcd->qcgd/dot_general | solution.py:113
  114.2 5.8 convolution_convert_fusion.1
  120.0 0.0 reduce-scatter.2.cloned.1.call-update
  120.1 0.7 copy-done.9
  120.7 0.1 copy.52
  120.8 0.1 eq.59
  120.9 0.1 reshape.420
  121.0 0.9 reduce-window.11
  121.9 0.2 slice_reduce_fusion
  122.2 0.1 fusion.44
  122.3 34.2 %reduce-scatter.2.cloned.1.call-done = bf16[96,2880]{1,0:T(8,128)(2,1)} async-done(((bf16[768,2880]{1,0:T(8,128)(2,1)}), bf16[96,2880]{1,0:T(8,128)(2,1)}) %reduce-scatter.2.cloned.1.call-update) | async-done | bytes 552976 | tf_op jit(solution)/shard_map/reduce_scatter | solution.py:115
  156.5 1.3 fusion.23
  157.9 1.3 fusion.25
  159.1 0.6 broadcast_in_dim.40
  159.7 2.4 reshape.422
  162.2 4.7 convolution_convert_fusion.2
  166.9 4.4 broadcast_in_dim.41
  171.3 7.1 %broadcast_in_dim.42 = bf16[32,4,14,2880]{3,2,1,0:T(8,128)(2,1)} broadcast(bf16[32,14,2880]{2,1,0:T(8,128)(2,1)} %broadcast_in_dim.41), dimensions={0,2,3} | broadcast | bytes 12902400 | tf_op jit(solution)/shard_map/broadcast_in_dim | solution.py:142
  178.4 146.2 %all_to_all.19 = bf16[128,14,2880]{2,1,0:T(8,128)(2,1)} all-to-all(bf16[128,14,2880]{2,1,0:T(8,128)(2,1)} %bitcast.109), channel_id=1, replica_groups=mesh['req'=16,'exp'=8] {'req','exp'}, dimensions={0} | all-to-all | bytes 20643840 | tf_op jit(solution)/shard_map/all_to_all | solution.py:145
  324.7 15.4 %reshape.424 = bf16[1792,2880]{1,0:T(8,128)(2,1)} reshape(bf16[128,14,2880]{2,1,0:T(8,128)(2,1)} %all_to_all.19) | data formatting | bytes 20643840 | tf_op jit(solution)/shard_map/reshape | solution.py:146
  340.0 14.6 %fusion.7 = f32[1792,720]{0,1:T(8,128)} fusion(bf16[1792,2880]{1,0:T(8,128)(2,1)} %reshape.424, bf16[1,2880,720]{1,2,0:T(8,128)(2,1)} %param.25), kind=kOutput, calls=%fused_computation.18 | convolution fusion | flops 7431782400 | bytes 19630080 | tf_op jit(solution)/shard_map/dot_general | solution.py:147
  354.6 27.2 %convolution_convert_fusion = bf16[1792,2880]{0,1:T(8,128)(2,1)} fusion(bf16[1,720,2880]{2,1,0:T(8,128)(2,1)} %param.27, f32[1792,720]{0,1:T(8,128)} %fusion.7, bf16[1792,2880]{1,0:T(8,128)(2,1)} %reshape.424, bf16[1,2880,720]{1,2,0:T(8,128)(2,1)} %param.26), kind=kOutput, calls=%fused_computation.10 | convolution fusion | flops 14879047680 | bytes 34099200 | tf_op jit(solution)/shard_map/dot_general | solution.py:150
  381.8 14.3 %copy.57 = bf16[1792,2880]{1,0:T(8,128)(2,1)} copy(bf16[1792,2880]{0,1:T(8,128)(2,1)} %convolution_convert_fusion) | data formatting | bytes 20643840 | tf_op jit(solution)/shard_map/convert_element_type | solution.py:150
  396.2 14.4 %reshape.425 = bf16[128,14,2880]{2,1,0:T(8,128)(2,1)} reshape(bf16[1792,2880]{1,0:T(8,128)(2,1)} %copy.57) | data formatting | bytes 20643840 | tf_op jit(solution)/shard_map/reshape | solution.py:154
  410.6 8.2 %all-to-all-start.2 = ((bf16[128,14,2880]{2,1,0:T(8,128)(2,1)}), bf16[128,14,2880]{2,1,0:T(8,128)(2,1)}, u32[]{:S(2)}, u32[]{:S(2)}) async-start(bf16[128,14,2880]{2,1,0:T(8,128)(2,1)} %reshape.425), calls=%async_computation.3 | async-start | bytes 24117248 | tf_op jit(solution)/shard_map/all_to_all | solution.py:153
  418.8 0.1 reduce_sum.92
  418.9 0.1 copy.49
  419.0 0.1 reshape.439
  419.1 0.1 copy.58
  419.3 0.1 mul.250
  419.4 0.1 copy.55
  419.5 0.1 copy.56
  419.6 0.3 fusion.60
  419.9 2.9 gather_fusion.1
  422.8 0.1 reshape.442
  422.9 0.1 copy.50
  423.1 0.7 copy.51
  423.8 143.8 %all-to-all-done.2 = bf16[128,14,2880]{2,1,0:T(8,128)(2,1)} async-done(((bf16[128,14,2880]{2,1,0:T(8,128)(2,1)}), bf16[128,14,2880]{2,1,0:T(8,128)(2,1)}, u32[]{:S(2)}, u32[]{:S(2)}) %all-to-all-start.2) | async-done | bytes 10321952 | tf_op jit(solution)/shard_map/all_to_all | solution.py:153
  567.6 9.8 %convert_reduce_fusion = f32[32,14,2880]{2,1,0:T(8,128)} fusion(bf16[128,14,2880]{2,1,0:T(8,128)(2,1)} %all-to-all-done.2), kind=kLoop, calls=%fused_computation.2 | loop fusion | flops 9031680 | bytes 15482880 | tf_op jit(solution)/shard_map/reduce_sum | solution.py:156
  577.4 5.6 reshape.428
  583.0 9.1 %gather_fusion = f32[384,2880]{1,0:T(8,128)} fusion(f32[448,2880]{1,0:T(8,128)} %reshape.428, s32[1024]{0:T(1024)S(1)} %pad_clamp_fusion), kind=kCustom, calls=%fused_computation | custom fusion | bytes 8848896 | tf_op jit(solution)/shard_map/jit(_take)/gather | solution.py:158
  592.1 5.5 gather.12
  597.6 6.5 %multiply_reduce_fusion = f32[96,2880]{1,0:T(8,128)S(1)} fusion(f32[96,4,2880]{2,1,0:T(4,128)} %gather.12, f32[96,4]{1,0:T(8,128)} %copy.51, pred[96,4]{1,0:T(8,128)(4,1)S(1)} %copy.56), kind=kLoop, calls=%fused_computation.15 | loop fusion | flops 3041280 | bytes 5531520 | tf_op jit(solution)/shard_map/reduce_sum | solution.py:159
  604.1 1.0 fusion.26
  (40 shorter events, 0.2 us)
Async XLA Ops:
  6.5 107.7 %copy-start = (bf16[512,2880]{0,1:T(8,128)(2,1)S(1)}, bf16[512,2880]{0,1:T(8,128)(2,1)}, u32[]{:S(2)}) copy-start(bf16[512,2880]{0,1:T(8,128)(2,1)} %param.20) | copy-start | bytes 8847364
  11.6 56.8 %all-to-all-start = ((bf16[8,96,2880]{2,1,0:T(8,128)(2,1)}), bf16[8,96,2880]{2,1,0:T(8,128)(2,1)}, u32[]{:S(2)}, u32[]{:S(2)}) async-start(bf16[8,96,2880]{2,1,0:T(8,128)(2,1)} %tile.2), calls=%async_computation | async-start | bytes 9043968 | tf_op jit(solution)/shard_map/all_to_all | solution.py:19
  16.5 4.6 copy-start.12
  16.5 140.0 %reduce-scatter.2.cloned.1.call-start = ((), (), s32[]{:S(2)}) async-start(), calls=%async_computation.4 | async-start | bytes 5087232 | tf_op jit(solution)/shard_map/reduce_scatter | solution.py:115
  68.4 4.4 copy-start.4
  72.7 5.0 copy-start.5
  72.7 5.0 copy-start.6
  78.0 8.8 %copy-start.11 = (f32[8]{0:T(128)S(1)}, f32[8]{0:T(128)}, u32[]{:S(2)}) copy-start(f32[8]{0:T(128)} %param.19) | copy-start | bytes 100
  86.2 0.6 copy-start.7
  120.0 0.7 copy-start.9
  120.0 36.5 %copy-start.2 = (bf16[96,2880]{1,0:T(8,128)(2,1)S(1)}, bf16[96,2880]{1,0:T(8,128)(2,1)}, u32[]{:S(2)}) copy-start(bf16[96,2880]{1,0:T(8,128)(2,1)} %param.14) | copy-start | bytes 1658884
  120.0 37.8 %copy-start.10 = (f32[2880]{0:T(1024)S(1)}, f32[2880]{0:T(1024)}, u32[]{:S(2)}) copy-start(f32[2880]{0:T(1024)} %param.21) | copy-start | bytes 34564
  410.6 9.0 %copy-start.8 = (bf16[2880,32]{0,1:T(8,128)(2,1)S(1)}, bf16[2880,32]{0,1:T(8,128)(2,1)}, u32[]{:S(2)}) copy-start(bf16[2880,32]{0,1:T(8,128)(2,1)} %param.22) | copy-start | bytes 552964
  410.6 157.0 %all-to-all-start.2 = ((bf16[128,14,2880]{2,1,0:T(8,128)(2,1)}), bf16[128,14,2880]{2,1,0:T(8,128)(2,1)}, u32[]{:S(2)}, u32[]{:S(2)}) async-start(bf16[128,14,2880]{2,1,0:T(8,128)(2,1)} %reshape.425), calls=%async_computation.3 | async-start | bytes 24117248 | tf_op jit(solution)/shard_map/all_to_all | solution.py:153
  592.1 13.1 %copy-start.1 = (bf16[512,2880]{0,1:T(8,128)(2,1)S(1)}, bf16[512,2880]{0,1:T(8,128)(2,1)}, u32[]{:S(2)}) copy-start(bf16[512,2880]{0,1:T(8,128)(2,1)} %param.20) | copy-start | bytes 8847364
  597.6 6.5 %copy-start.3 = (bf16[96,2880]{1,0:T(8,128)(2,1)S(1)}, bf16[96,2880]{1,0:T(8,128)(2,1)}, u32[]{:S(2)}) copy-start(bf16[96,2880]{1,0:T(8,128)(2,1)} %reduce-scatter.2.cloned.1.call-done) | copy-start | bytes 1658884
Sparse Core Ops, SparseCore 0:
  120.2 36.2 reduce-scatter.1
